TPU v7x, 32 devices: a whole 2x2x4 slice. The times are simulated.
32 devices in a mesh: dp: 4 (over x, core), pipe: 2 (over y), tensor: 4 (over z).
Axes of the slice: x: 2, y: 2, z: 4, core: 2. Of those that a mesh axis runs over, the one named last changes fastest.
Arguments:
- layer_input: bfloat16 [4, 2, 512, 8192], P('dp', 'pipe', None, 'tensor'), may hold values from -40 to 40
- output_grad: bfloat16 [4, 2, 512, 8192], P('dp', 'pipe', None, 'tensor'), may hold values from -6 to 6
- kv_grad: bfloat16 [4, 2, 512, 2048], P('dp', 'pipe', None, 'tensor'), may hold values from -6 to 6
- norm_gain: bfloat16 [2, 8192], P('pipe', 'tensor'), may hold values from 0.5 to 1.5
- kv_weight: bfloat16 [2, 8192, 2048], P('pipe', 'tensor'), may hold values from -0.0625 to 0.0625
Outputs:
- upstream_grad: bfloat16 [4, 2, 512, 8192], P('dp', 'pipe', None, 'tensor')
- kv_weight_grad: bfloat16 [2, 8192, 2048], P('pipe', 'tensor', 'dp')
- gain_grad: float32 [2, 8192], P('pipe', 'tensor')
All inputs are finite; a program needn't handle non-finite values.
Results may differ from a plain program's by a relative error of at most 0.009.
Values may be sent and summed in bfloat16 or wider, within the bound.
No kernel may reach another device: no remote copies, remote signals or barrier semaphores. Data moves between devices by JAX's collectives and lax.ppermute only.
A program may use at most 128 MiB of HBM per device.

v0:
```python
import jax
import jax.numpy as jnp
from jax import lax
from jax.sharding import PartitionSpec as P

D = 8192


def from_behind(block, axis, distance):
    devices = range(lax.axis_size(axis))
    route = [(i - distance, i) for i in devices if i - distance in devices]
    return lax.ppermute(block, axis, route)


def on_device(layer_input, output_grad, kv_grad, norm_gain, kv_weight):
    rows = layer_input[0, 0]
    grad_out = output_grad[0, 0]
    grad_kv = kv_grad[0, 0]
    gain_f = norm_gain[0].astype(jnp.float32)
    weight = kv_weight[0]
    values = rows.astype(jnp.float32)
    local_squares = jnp.sum(values * values, axis=1, keepdims=True)
    total_squares = lax.psum(local_squares, "tensor")
    rstd = lax.rsqrt(total_squares / D + 1e-05)
    normed = values * rstd
    hidden = (normed * gain_f).astype(jnp.bfloat16)
    piece = lax.all_gather(grad_kv, "tensor", axis=1, tiled=True)
    row_total = lax.dot_general(
        piece, weight, (((1,), (1,)), ((), ())), preferred_element_type=jnp.float32
    )
    term = lax.dot_general(
        hidden, piece, (((0,), (0,)), ((), ())), preferred_element_type=jnp.float32
    )
    weight_total = term
    wgrad = weight_total
    scaled = gain_f * row_total
    local_dot = jnp.sum(scaled * normed, axis=1, keepdims=True)
    mean_term = lax.psum(local_dot, "tensor") / D
    input_grad = (grad_out.astype(jnp.float32) + rstd * (scaled - normed * mean_term)).astype(
        jnp.bfloat16
    )
    upstream = from_behind(input_grad, "pipe", -1)
    gain_part = jnp.sum(row_total * normed, axis=0)
    gain_total = lax.psum(gain_part, "dp")
    weight_total = lax.psum_scatter(
        wgrad.astype(jnp.bfloat16), "dp", scatter_dimension=1, tiled=True
    )
    return (upstream[None, None], weight_total[None], gain_total[None])


def solution(mesh):
    in_specs = (
        P("dp", "pipe", None, "tensor"),
        P("dp", "pipe", None, "tensor"),
        P("dp", "pipe", None, "tensor"),
        P("pipe", "tensor"),
        P("pipe", "tensor", None),
    )
    out_specs = (P("dp", "pipe", None, "tensor"), P("pipe", "tensor", "dp"), P("pipe", "tensor"))
    return jax.shard_map(
        on_device, mesh=mesh, in_specs=in_specs, out_specs=out_specs, check_vma=False
    )
```

profile of v0, /device:TPU:0, one launch (start us, length us, event | category | flops | bytes accessed | tf_op | source)
XLA Modules:
  0.0 152.9 jit_solution(5806783644709270451)
XLA Ops:
  7.2 0.0 all-gather.3.cloned.1.call-start
  7.2 0.7 all-gather.3.cloned.1.call-update
  7.9 0.0 reduce-scatter.2.cloned.1.call-start
  7.9 0.7 mul.69
  8.7 2.1 %fusion.13 = f32[512]{0:T(512)S(1)} fusion(bf16[1,1,512,2048]{3,2,1,0:T(8,128)(2,1)} %param.5), kind=kLoop, calls=%fused_computation.16 | loop fusion | flops 3145216 | bytes 2099200 | tf_op jit(solution)/shard_map/reduce_sum | solution.py:22
  10.7 13.7 %psum.21 = f32[512,1]{0,1:T(1,128)S(1)} all-reduce(f32[512,1]{0,1:T(1,128)S(1)} %bitcast.37), channel_id=1, replica_groups=mesh['dp'=4,'pipe'=2,'tensor'=4] {'tensor'}, use_global_device_ids=true, to_apply=%region_1.0 | all-reduce | flops 512 | bytes 4096 | tf_op jit(solution)/shard_map/psum | solution.py:23
  24.4 33.9 %all-gather.3.cloned.1.call-done = bf16[1,1,512,2048]{3,2,1,0:T(8,128)(2,1)} async-done(((bf16[1,1,512,512]{3,2,1,0:T(8,128)(2,1)}), bf16[1,1,512,2048]{3,2,1,0:T(8,128)(2,1)}) %all-gather.3.cloned.1.call-update) | async-done | bytes 2097168 | tf_op jit(solution)/shard_map/all_gather | solution.py:27
  58.3 10.1 %convolution_convert_fusion = bf16[2048,2048]{1,0:T(8,128)(2,1)} fusion(bf16[1,1,512,2048]{3,2,1,0:T(8,128)(2,1)} %param.5, bf16[1,1,512,2048]{3,2,1,0:T(8,128)(2,1)} %all-gather.3.cloned.1.call-done, f32[2048]{0:T(1024)S(1)} %bitcast.34, f32[512]{0:T(512)S(1)} %bitcast.39), kind=kOutput, calls=%fused_computation.2 | convolution fusion | flops 4303355904 | bytes 12593152 | tf_op jit(solution)/shard_map/dot_general | solution.py:31
  68.4 0.0 copy-start
  68.4 0.0 reduce-scatter.2.cloned.1.call-update
  68.4 1.6 %copy-done = bf16[1,1,512,2048]{3,2,1,0:T(8,128)(2,1)S(1)} copy-done((bf16[1,1,512,2048]{3,2,1,0:T(8,128)(2,1)S(1)}, bf16[1,1,512,2048]{3,2,1,0:T(8,128)(2,1)}, u32[]{:S(2)}) %copy-start) | copy-done | bytes 2097176
  70.0 11.8 %fusion.12 = (f32[2048]{0:T(1024)S(1)}, f32[512]{0:T(512)S(1)}, f32[512,2048]{1,0:T(8,128)}) fusion(bf16[1,1,512,2048]{3,2,1,0:T(8,128)(2,1)S(1)} %copy-done, f32[512]{0:T(512)S(1)} %bitcast.40, f32[2048]{0:T(1024)S(1)} %bitcast.35, bf16[1,2048,2048]{2,1,0:T(8,128)(2,1)} %param.9, bf16[1,1,512,2048]{3,2,1,0:T(8,128)(2,1)} %all-gather.3.cloned.1.call-done), kind=kOutput, calls=%fused_computation.15 | convolution fusion | flops 4302304768 | bytes 16797696 | tf_op jit(solution)/shard_map/dot_general | solution.py:28
  81.8 9.0 %psum.22 = f32[512,1]{0,1:T(1,128)S(1)} all-reduce(f32[512,1]{0,1:T(1,128)S(1)} %bitcast.43), channel_id=1, replica_groups=mesh['dp'=4,'pipe'=2,'tensor'=4] {'tensor'}, use_global_device_ids=true, to_apply=%region_3.0 | all-reduce | flops 512 | bytes 4096 | tf_op jit(solution)/shard_map/psum | solution.py:38
  90.8 5.7 %fusion.10 = bf16[512,2048]{1,0:T(8,128)(2,1)} fusion(f32[512,2048]{1,0:T(8,128)} %get-tuple-element.5, bf16[1,1,512,2048]{3,2,1,0:T(8,128)(2,1)} %param.6, bf16[1,1,512,2048]{3,2,1,0:T(8,128)(2,1)S(1)} %copy-done, f32[512]{0:T(512)S(1)} %bitcast.42, f32[2048]{0:T(1024)S(1)} %bitcast.36, f32[512]{0:T(512)S(1)} %bitcast.41), kind=kLoop, calls=%fused_computation.13 | loop fusion | flops 9437184 | bytes 10498048 | tf_op jit(solution)/shard_map/convert_element_type | solution.py:39
  96.5 1.3 collective-permute-start
  97.8 7.0 %psum.23 = f32[1,2048]{1,0:T(1,128)} all-reduce(f32[1,2048]{1,0:T(1,128)S(1)} %bitcast.38), channel_id=1, replica_groups=mesh['dp'=4,'pipe'=2,'tensor'=4] {'dp'}, use_global_device_ids=true, to_apply=%region_6.0 | all-reduce | flops 2048 | bytes 16384 | tf_op jit(solution)/shard_map/psum | solution.py:44
  104.8 39.9 %collective-permute-done = bf16[512,2048]{1,0:T(8,128)(2,1)S(1)} collective-permute-done((bf16[512,2048]{1,0:T(8,128)(2,1)}, bf16[512,2048]{1,0:T(8,128)(2,1)S(1)}, u32[]{:S(2)}, u32[]{:S(2)}) %collective-permute-start) | collective-permute-done | bytes 2097184 | tf_op jit(solution)/shard_map/ppermute | solution.py:12
  144.7 0.0 reduce-scatter.2.cloned.1.call-done
  144.7 1.3 copy.9
  (2 shorter events, 0.0 us)
Async XLA Ops:
  7.2 51.1 %all-gather.3.cloned.1.call-start = ((), (), s32[]{:S(2)}) async-start(), calls=%async_computation.2 | async-start | bytes 2621440 | tf_op jit(solution)/shard_map/all_gather | solution.py:27
  7.9 136.8 %reduce-scatter.2.cloned.1.call-start = ((), (), s32[]{:S(2)}) async-start(), calls=%async_computation.1 | async-start | bytes 10485760 | tf_op jit(solution)/shard_map/reduce_scatter | solution.py:45
  68.4 1.6 %copy-start = (bf16[1,1,512,2048]{3,2,1,0:T(8,128)(2,1)S(1)}, bf16[1,1,512,2048]{3,2,1,0:T(8,128)(2,1)}, u32[]{:S(2)}) copy-start(bf16[1,1,512,2048]{3,2,1,0:T(8,128)(2,1)} %param.5) | copy-start | bytes 6291460
  96.5 48.2 %collective-permute-start = (bf16[512,2048]{1,0:T(8,128)(2,1)}, bf16[512,2048]{1,0:T(8,128)(2,1)S(1)}, u32[]{:S(2)}, u32[]{:S(2)}) collective-permute-start(bf16[512,2048]{1,0:T(8,128)(2,1)} %fusion.10), channel_id=1, source_target_pairs={{4,0},{5,1},{6,2},{7,3},{12,8},{13,9},{14,10},{15,11},{20,16},{21,... | collective-permute-start | bytes 6291464 | tf_op jit(solution)/shard_map/ppermute | solution.py:12
Sparse Core Ops, SparseCore 0:
  9.6 48.6 all-gather.2
  68.5 70.6 reduce-scatter.1
where the time goes:
time: 153 us
  waiting for transfers between devices  74.5 us (49%)
  blocking collectives  29.6 us (19%)
  matrix products  21.9 us (14%)
  between operations  14.1 us (9%)
  other arithmetic  8.53 us (6%)
  local copies, waits for them, and re-layouts  2.89 us (2%)
    ppermute x1, waiting for transfers between devices, from_behind(): return lax.ppermute(block, axis, route)  39.9 us
    all_gather x1, waiting for transfers between devices, on_device(): piece = lax.all_gather(grad_kv, 'tensor', axis=1, tiled=True)  33.9 us
    psum x1, blocking collectives, on_device(): total_squares = lax.psum(local_squares, 'tensor')  13.7 us
    dot_general x1, matrix products, on_device(): lax.dot_general(piece, weight, (((1,), (1,)), ((), ())), preferred_elemen...  11.8 us
    dot_general x1, matrix products, on_device(): lax.dot_general(hidden, piece, (((0,), (0,)), ((), ())), preferred_elemen...  10.1 us
    psum x1, blocking collectives, on_device(): mean_term = lax.psum(local_dot, 'tensor') / D  8.96 us
    psum x1, blocking collectives, on_device(): gain_total = lax.psum(gain_part, 'dp')  7.03 us
    convert_element_type x1, other arithmetic, on_device(): (grad_out.astype(jnp.float32) + rstd * (scaled - normed * mean_term)).ast...  5.73 us
  transfers between devices with their start and end apart: 3, of which 2 were waited for; matrix products, arithmetic and copies ran while one was open for 13% of the time, Pallas kernels for 0%

commit v1 on v0

--- a/solution.py
+++ b/solution.py
@@ -24,7 +24,23 @@
     rstd = lax.rsqrt(total_squares / D + 1e-05)
     normed = values * rstd
     hidden = (normed * gain_f).astype(jnp.bfloat16)
-    piece = lax.all_gather(grad_kv, "tensor", axis=1, tiled=True)
+    size, index, span = (lax.axis_size("tensor"), lax.axis_index("tensor"), grad_kv.shape[1])
+    upward = [(i_2, (i_2 + 1) % size) for i_2 in range(size)]
+    backward = [(i_2, (i_2 - 1) % size) for i_2 in range(size)]
+    piece = jnp.zeros((*grad_kv.shape[:1], size * span, *grad_kv.shape[1 + 1 :]), grad_kv.dtype)
+    piece = lax.dynamic_update_slice_in_dim(piece, grad_kv, index * span, axis=1)
+    from_left = from_right = grad_kv
+    middle = size // 2
+    for step in range(1, middle + 1):
+        from_left = lax.ppermute(from_left, "tensor", upward)
+        piece = lax.dynamic_update_slice_in_dim(
+            piece, from_left, (index - step) % size * span, axis=1
+        )
+        if step < size - middle:
+            from_right = lax.ppermute(from_right, "tensor", backward)
+            piece = lax.dynamic_update_slice_in_dim(
+                piece, from_right, (index + step) % size * span, axis=1
+            )
     row_total = lax.dot_general(
         piece, weight, (((1,), (1,)), ((), ())), preferred_element_type=jnp.float32
     )

time: 153 us -> 141 us (0.922)
  waiting for transfers between devices: 74.5 us -> 47.1 us
  blocking collectives: 29.6 us -> 40.1 us
  starting transfers between devices: 1.36 us -> 6.81 us
  matrix products: 21.9 us -> 18.4 us
  local copies, waits for them, and re-layouts: 2.89 us -> 5.2 us
    all_gather x1 -> x0, waiting for transfers between devices: 33.9 us -> none  [on_device(): piece = lax.all_gather(grad_kv, 'tensor', axis=1, tiled=True)]
    ppermute x0 -> x3, waiting for transfers between devices: none -> 11.2 us  [the longest x2 11.2 us: on_device(): from_left = lax.ppermute(from_left, 'tensor', upward)]
    psum x1, blocking collectives: 13.7 us -> 24.7 us  [on_device(): total_squares = lax.psum(local_squares, 'tensor')]
    ppermute x0 -> x3, starting transfers between devices: none -> 5.49 us  [the longest x2 3.4 us: on_device(): from_left = lax.ppermute(from_left, 'tensor', upward)]
    ppermute x1, waiting for transfers between devices: 39.9 us -> 35.7 us  [from_behind(): return lax.ppermute(block, axis, route)]
    dot_general x1, matrix products: 10.1 us -> 6.93 us  [on_device(): lax.dot_general(hidden, piece, (((0,), (0,)), ((), ())), preferred_elemen...]
    dynamic_update_slice x0 -> x4, local copies, waits for them, and re-layouts: none -> 2.32 us  [the longest x2 1.16 us: on_device(): lax.dynamic_update_slice_in_dim(piece, from_left, (index - step) % size *...]
  transfers between devices with their start and end apart: 3 -> 5, of which waited for: 2 -> 3; matrix products, arithmetic and copies ran while one was open for 13% -> 16% of each run, Pallas kernels for 0% -> 0%
where the time goes in v1:
time: 141 us
  waiting for transfers between devices  47.1 us (33%)
  blocking collectives  40.1 us (28%)
  matrix products  18.4 us (13%)
  between operations  14.2 us (10%)
  other arithmetic  9.06 us (6%)
  starting transfers between devices  6.81 us (5%)
  local copies, waits for them, and re-layouts  5.2 us (4%)
    ppermute x1, waiting for transfers between devices, from_behind(): return lax.ppermute(block, axis, route)  35.7 us
    psum x1, blocking collectives, on_device(): total_squares = lax.psum(local_squares, 'tensor')  24.7 us
    dot_general x1, matrix products, on_device(): lax.dot_general(piece, weight, (((1,), (1,)), ((), ())), preferred_elemen...  11.5 us
    ppermute x2, waiting for transfers between devices, on_device(): from_left = lax.ppermute(from_left, 'tensor', upward)  11.2 us
    psum x1, blocking collectives, on_device(): mean_term = lax.psum(local_dot, 'tensor') / D  8.34 us
    psum x1, blocking collectives, on_device(): gain_total = lax.psum(gain_part, 'dp')  7.03 us
    dot_general x1, matrix products, on_device(): lax.dot_general(hidden, piece, (((0,), (0,)), ((), ())), preferred_elemen...  6.93 us
    convert_element_type x1, other arithmetic, on_device(): (grad_out.astype(jnp.float32) + rstd * (scaled - normed * mean_term)).ast...  6.26 us
  transfers between devices with their start and end apart: 5, of which 3 were waited for; matrix products, arithmetic and copies ran while one was open for 16% of the time, Pallas kernels for 0%

profile of v1, /device:TPU:0, one launch (start us, length us, event | category | flops | bytes accessed | tf_op | source)
XLA Modules:
  0.0 140.9 jit_solution(1324864764677390761)
XLA Ops:
  7.2 0.0 reduce-scatter.2.cloned.1.call-start
  7.2 3.1 %collective-permute-start = (bf16[512,512]{1,0:T(8,128)(2,1)}, bf16[512,512]{1,0:T(8,128)(2,1)S(1)}, u32[]{:S(2)}, u32[]{:S(2)}) collective-permute-start(bf16[512,512]{1,0:T(8,128)(2,1)} %bitcast.31), channel_id=1, source_target_pairs={{0,1},{1,2},{2,3},{3,0},{4,5},{5,6},{6,7},{7,4},{8,9},{9,10},{10,1... | collective-permute-start | bytes 1572872 | tf_op jit(solution)/shard_map/ppermute | solution.py:35
  10.3 2.1 %collective-permute-start.1 = (bf16[512,512]{1,0:T(8,128)(2,1)}, bf16[512,512]{1,0:T(8,128)(2,1)}, u32[]{:S(2)}, u32[]{:S(2)}) collective-permute-start(bf16[512,512]{1,0:T(8,128)(2,1)} %bitcast.32), channel_id=1, source_target_pairs={{0,3},{1,0},{2,1},{3,2},{4,7},{5,4},{6,5},{7,6},{8,11},{9,8},{10,9... | collective-permute-start | bytes 1572872 | tf_op jit(solution)/shard_map/ppermute | solution.py:40
  12.4 2.1 %fusion.13 = f32[512]{0:T(512)S(1)} fusion(bf16[1,1,512,2048]{3,2,1,0:T(8,128)(2,1)} %param.5), kind=kLoop, calls=%fused_computation.16 | loop fusion | flops 3145216 | bytes 2099200 | tf_op jit(solution)/shard_map/reduce_sum | solution.py:22
  14.5 24.7 %psum.21 = f32[512,1]{0,1:T(1,128)S(1)} all-reduce(f32[512,1]{0,1:T(1,128)S(1)} %bitcast.36), channel_id=1, replica_groups=mesh['dp'=4,'pipe'=2,'tensor'=4] {'tensor'}, use_global_device_ids=true, to_apply=%region_1.0 | all-reduce | flops 512 | bytes 4096 | tf_op jit(solution)/shard_map/psum | solution.py:23
  39.2 0.3 collective-permute-start.2
  39.6 0.7 mul.85
  40.3 0.2 broadcast_in_dim.21
  40.6 0.1 constant_dynamic-update-slice_fusion.3
  40.7 0.1 constant_dynamic-update-slice_fusion.2
  40.8 1.1 constant_dynamic-update-slice_fusion.1
  41.9 11.1 %collective-permute-done.2 = bf16[512,512]{1,0:T(8,128)(2,1)} collective-permute-done((bf16[512,512]{1,0:T(8,128)(2,1)S(1)}, bf16[512,512]{1,0:T(8,128)(2,1)}, u32[]{:S(2)}, u32[]{:S(2)}) %collective-permute-start.2) | collective-permute-done | bytes 524320 | tf_op jit(solution)/shard_map/ppermute | solution.py:35
  53.0 1.1 constant_dynamic-update-slice_fusion
  54.1 1.3 copy-done.1
  55.4 6.9 %convolution_convert_fusion = bf16[2048,2048]{1,0:T(8,128)(2,1)} fusion(bf16[512,2048]{1,0:T(8,128)(2,1)S(1)} %constant_dynamic-update-slice_fusion, bf16[1,1,512,2048]{3,2,1,0:T(8,128)(2,1)S(1)} %copy-done, f32[2048]{0:T(1024)S(1)} %bitcast.33, f32[512]{0:T(512)S(1)} %bitcast.38), kind=kOutput, calls=%fused_computation.2 | convolution fusion | flops 4303355904 | bytes 12593152 | tf_op jit(solution)/shard_map/dot_general | solution.py:47
  62.4 0.0 reduce-scatter.2.cloned.1.call-update
  62.4 11.5 %fusion.12 = (f32[2048]{0:T(1024)S(1)}, f32[512]{0:T(512)S(1)}, f32[512,2048]{1,0:T(8,128)}) fusion(bf16[1,1,512,2048]{3,2,1,0:T(8,128)(2,1)S(1)} %copy-done, f32[512]{0:T(512)S(1)} %bitcast.39, f32[2048]{0:T(1024)S(1)} %bitcast.34, bf16[512,2048]{1,0:T(8,128)(2,1)} %copy-done.1, bf16[1,2048,2048]{2,1,0:T(8,128)(2,1)} %param.9), kind=kOutput, calls=%fused_computation.15 | convolution fusion | flops 4302304768 | bytes 16797696 | tf_op jit(solution)/shard_map/dot_general | solution.py:44
  73.9 8.3 %psum.22 = f32[512,1]{0,1:T(1,128)S(1)} all-reduce(f32[512,1]{0,1:T(1,128)S(1)} %bitcast.42), channel_id=1, replica_groups=mesh['dp'=4,'pipe'=2,'tensor'=4] {'tensor'}, use_global_device_ids=true, to_apply=%region_3.4 | all-reduce | flops 512 | bytes 4096 | tf_op jit(solution)/shard_map/psum | solution.py:54
  82.3 6.3 %fusion.10 = bf16[512,2048]{1,0:T(8,128)(2,1)} fusion(f32[512,2048]{1,0:T(8,128)} %get-tuple-element.5, bf16[1,1,512,2048]{3,2,1,0:T(8,128)(2,1)} %param.6, bf16[1,1,512,2048]{3,2,1,0:T(8,128)(2,1)S(1)} %copy-done, f32[512]{0:T(512)S(1)} %bitcast.41, f32[2048]{0:T(1024)S(1)} %bitcast.35, f32[512]{0:T(512)S(1)} %bitcast.40), kind=kLoop, calls=%fused_computation.13 | loop fusion | flops 9437184 | bytes 10498048 | tf_op jit(solution)/shard_map/convert_element_type | solution.py:55
  88.5 1.3 collective-permute-start.3
  89.8 7.0 %psum.23 = f32[1,2048]{1,0:T(1,128)} all-reduce(f32[1,2048]{1,0:T(1,128)S(1)} %bitcast.37), channel_id=1, replica_groups=mesh['dp'=4,'pipe'=2,'tensor'=4] {'dp'}, use_global_device_ids=true, to_apply=%region_6.7 | all-reduce | flops 2048 | bytes 16384 | tf_op jit(solution)/shard_map/psum | solution.py:60
  96.8 35.7 %collective-permute-done.3 = bf16[512,2048]{1,0:T(8,128)(2,1)S(1)} collective-permute-done((bf16[512,2048]{1,0:T(8,128)(2,1)}, bf16[512,2048]{1,0:T(8,128)(2,1)S(1)}, u32[]{:S(2)}, u32[]{:S(2)}) %collective-permute-start.3) | collective-permute-done | bytes 2097184 | tf_op jit(solution)/shard_map/ppermute | solution.py:12
  132.6 0.2 reduce-scatter.2.cloned.1.call-done
  132.7 1.3 copy.13
  (9 shorter events, 0.0 us)
Async XLA Ops:
  7.2 33.4 %copy-start.2 = (bf16[1,1,512,512]{3,2,1,0:T(8,128)(2,1)S(1)}, bf16[1,1,512,512]{3,2,1,0:T(8,128)(2,1)}, u32[]{:S(2)}) copy-start(bf16[1,1,512,512]{3,2,1,0:T(8,128)(2,1)} %param.7) | copy-start | bytes 1572868
  7.2 125.6 %reduce-scatter.2.cloned.1.call-start = ((), (), s32[]{:S(2)}) async-start(), calls=%async_computation.1 | async-start | bytes 10485760 | tf_op jit(solution)/shard_map/reduce_scatter | solution.py:61
  7.2 48.2 %copy-start = (bf16[1,1,512,2048]{3,2,1,0:T(8,128)(2,1)S(1)}, bf16[1,1,512,2048]{3,2,1,0:T(8,128)(2,1)}, u32[]{:S(2)}) copy-start(bf16[1,1,512,2048]{3,2,1,0:T(8,128)(2,1)} %param.5) | copy-start | bytes 6291460
  7.2 32.0 %collective-permute-start = (bf16[512,512]{1,0:T(8,128)(2,1)}, bf16[512,512]{1,0:T(8,128)(2,1)S(1)}, u32[]{:S(2)}, u32[]{:S(2)}) collective-permute-start(bf16[512,512]{1,0:T(8,128)(2,1)} %bitcast.31), channel_id=1, source_target_pairs={{0,1},{1,2},{2,3},{3,0},{4,5},{5,6},{6,7},{7,4},{8,9},{9,10},{10,1... | collective-permute-start | bytes 1572872 | tf_op jit(solution)/shard_map/ppermute | solution.py:35
  10.3 30.4 %collective-permute-start.1 = (bf16[512,512]{1,0:T(8,128)(2,1)}, bf16[512,512]{1,0:T(8,128)(2,1)}, u32[]{:S(2)}, u32[]{:S(2)}) collective-permute-start(bf16[512,512]{1,0:T(8,128)(2,1)} %bitcast.32), channel_id=1, source_target_pairs={{0,3},{1,0},{2,1},{3,2},{4,7},{5,4},{6,5},{7,6},{8,11},{9,8},{10,9... | collective-permute-start | bytes 1572872 | tf_op jit(solution)/shard_map/ppermute | solution.py:40
  39.2 13.8 %collective-permute-start.2 = (bf16[512,512]{1,0:T(8,128)(2,1)S(1)}, bf16[512,512]{1,0:T(8,128)(2,1)}, u32[]{:S(2)}, u32[]{:S(2)}) collective-permute-start(bf16[512,512]{1,0:T(8,128)(2,1)S(1)} %collective-permute-done), channel_id=1, source_target_pairs={{0,1},{1,2},{2,3},{3,0},{4,5},{5,6},{6,7},{7,4},{8,9},{9,10},{10,1... | collective-permute-start | bytes 1572872 | tf_op jit(solution)/shard_map/ppermute | solution.py:35
  54.1 1.3 copy-start.1
  88.5 44.0 %collective-permute-start.3 = (bf16[512,2048]{1,0:T(8,128)(2,1)}, bf16[512,2048]{1,0:T(8,128)(2,1)S(1)}, u32[]{:S(2)}, u32[]{:S(2)}) collective-permute-start(bf16[512,2048]{1,0:T(8,128)(2,1)} %fusion.10), channel_id=1, source_target_pairs={{4,0},{5,1},{6,2},{7,3},{12,8},{13,9},{14,10},{15,11},{20,16},{21,... | collective-permute-start | bytes 6291464 | tf_op jit(solution)/shard_map/ppermute | solution.py:12
Sparse Core Ops, SparseCore 0:
  62.5 70.1 reduce-scatter.1
